TPU v7x, 256 devices: a whole 4x4x8 slice. The times are simulated.
256 devices in a mesh: seq: 16 (over y, z_hi, core), head: 16 (over x, z_lo).
Axes of the slice: x: 4, y: 4, z: 8 (z_hi: 2, z_lo: 4; z = z_hi * 4 + z_lo), core: 2. Of those that a mesh axis runs over, the one named last changes fastest.
Arguments:
- x_in: bfloat16 [8192, 8192], P('seq', 'head'), may hold values from -6 to 6
- z_in: bfloat16 [8192, 8192], P('seq', 'head'), may hold values from -12 to 12
- bc: bfloat16 [2, 8192, 128], P(None, 'seq'), may hold values from -1.796875 to 1.796875
- dt_raw: float32 [128, 8192], P('head', 'seq'), may hold values from -3 to 3
- dt_bias: float32 [128], P('head'), may hold values from -8 to 0
- decay_rate: float32 [128], P('head'), may hold values from 0.001 to 0.4
- d_skip: float32 [128], P('head'), may hold values from 0.5 to 1.5
- norm_gain: float32 [8192], P('head'), may hold values from 0.1 to 1.9
- out_weight: bfloat16 [8192, 4096], P('head', 'seq'), may hold values from -0.0625 to 0.0625
- resid: bfloat16 [8192, 4096], P(('seq', 'head')), may hold values from -6 to 6
- mlp_gain: float32 [4096], replicated, may hold values from 0.1 to 1.9
- gate_weight: bfloat16 [4096, 8192], P(None, 'head'), may hold values from -0.09375 to 0.09375
- up_weight: bfloat16 [4096, 8192], P(None, 'head'), may hold values from -0.09375 to 0.09375
- down_weight: bfloat16 [8192, 4096], P('head', 'seq'), may hold values from -0.0625 to 0.0625
Outputs:
- layer_out: bfloat16 [8192, 4096], P(('seq', 'head'))
All inputs are finite; a program needn't handle non-finite values.
Results may differ from a plain program's by a relative error of at most 0.0075.
Values may be sent and summed in bfloat16 or wider, within the bound.
No kernel may reach another device: no remote copies, remote signals or barrier semaphores. Data moves between devices by JAX's collectives and lax.ppermute only.
A program may use at most 128 MiB of HBM per device.

v0:
```python
import jax
import jax.numpy as jnp
from jax import lax
from jax.sharding import PartitionSpec as P

BLOCK = 256
INNER = 8192
epsilon = 1e-05
SEQ = ("sy", "sz", "sc")


def block_scan(x_heads, b_rows, c_rows, step_size, log_decay, block_len):
    length, head_count, head_width = x_heads.shape
    state_size = b_rows.shape[1]
    block_count = length // block_len
    lower_mask = jnp.tril(jnp.ones((block_len, block_len), dtype=bool))
    carry_state = jnp.zeros((head_count, head_width, state_size), jnp.float32)
    outs = []
    for blk in range(block_count):
        rows = slice(blk * block_len, (blk + 1) * block_len)
        x_block = x_heads[rows]
        b_block = b_rows[rows]
        c_block = c_rows[rows]
        d_block = step_size[:, rows]
        a_block = log_decay[:, rows]
        cumulative = jnp.cumsum(a_block, axis=1)
        gap_values = jnp.where(
            lower_mask[None], cumulative[:, :, None] - cumulative[:, None, :], -jnp.inf
        )
        scores = jnp.dot(c_block, b_block.T, preferred_element_type=jnp.float32)
        mixing = (jnp.exp(gap_values) * scores[None] * d_block[:, None, :]).astype(jnp.bfloat16)
        within = jnp.einsum("hij,jhp->ihp", mixing, x_block, preferred_element_type=jnp.float32)
        if blk > 0:
            carried = jnp.einsum(
                "in,hpn->ihp",
                c_block.astype(jnp.float32),
                carry_state,
                precision=lax.Precision.HIGHEST,
            )
            within = within + carried * jnp.exp(cumulative).T[:, :, None]
        last_cum = cumulative[:, -1:]
        inject = (
            (jnp.exp(last_cum - cumulative) * d_block)[:, :, None]
            * b_block.astype(jnp.float32)[None]
        ).astype(jnp.bfloat16)
        added = jnp.einsum("jhp,hjn->hpn", x_block, inject, preferred_element_type=jnp.float32)
        carry_state = jnp.exp(last_cum)[:, :, None] * carry_state + added
        outs.append(within)
    return (jnp.concatenate(outs, axis=0), carry_state)


def combine(first, second):
    (d1, s1), (d2, s2) = (first, second)
    return (d1 * d2, d2[:, None, None] * s1 + s2)


def send(pair, pairs, axes):
    return tuple((lax.ppermute(v, axes, pairs) for v in pair))


def entering_state(group_decay, local_state):
    block = ("sz", "sc")
    j = lax.axis_index("sz") * 2 + lax.axis_index("sc")
    y = lax.axis_index("sy")
    ny = lax.axis_size("sy")
    own = (group_decay, local_state)
    ident = (jnp.ones_like(group_decay), jnp.zeros_like(local_state))

    def pick(cond, a, b):
        return tuple((jnp.where(cond, u, v) for u, v in zip(a, b)))

    got = send(own, [(0, 1), (2, 3)], block)
    pair_agg = combine(got, own)
    lower = send(pair_agg, [(1, 2)], block)
    lower3 = send(lower, [(2, 3)], block)
    inner = pick(j == 1, got, ident)
    inner = pick(j == 2, lower, inner)
    inner = pick(j == 3, combine(lower3, got), inner)
    block_agg = combine(lower3, pair_agg)
    full = SEQ
    before = ident
    for k in range(ny - 1, 0, -1):
        pairs = [(4 * src + 3, 4 * (src + k) + 3) for src in range(ny - k)]
        got_k = send(block_agg, pairs, full)
        before = combine(before, pick(y >= k, got_k, ident))
    to_2 = send(before, [(3, 2)], block)
    to_1 = send(before, [(3, 1)], block)
    to_0 = send(to_1, [(1, 0)], block)
    prefix = pick(j == 3, before, to_0)
    prefix = pick(j == 2, to_2, prefix)
    prefix = pick(j == 1, to_1, prefix)
    return combine(prefix, inner)[1]


def ring_sum_x(pieces):
    nx = pieces.shape[0]
    x = lax.axis_index("hx")
    half = pieces.shape[2] // 2
    ways = ((1, pieces[:, :, :half]), (-1, pieces[:, :, half:]))
    accs = []
    for way, part in ways:
        pairs = [(src, (src + way) % nx) for src in range(nx)]
        acc = jnp.take(part, (x - way) % nx, axis=0).astype(jnp.float32)
        for step in range(nx - 1):
            got = lax.ppermute(acc.astype(jnp.bfloat16), "hx", pairs)
            chunk = (x - way * (step + 2)) % nx
            acc = got.astype(jnp.float32) + jnp.take(part, chunk, axis=0).astype(jnp.float32)
        accs.append(acc)
    return jnp.concatenate(accs, axis=1)


def sum_over_head(value):
    nx, nz = (lax.axis_size("hx"), lax.axis_size("hz"))
    pieces = value.reshape(nx, nz, value.shape[0] // (nx * nz), value.shape[1])
    pieces = ring_sum_x(pieces).astype(jnp.bfloat16)
    pieces = lax.all_to_all(pieces, "hz", 0, 0, tiled=False)
    return jnp.sum(pieces.astype(jnp.float32), axis=0)


def ring_gather_x(value):
    nx = lax.axis_size("hx")
    x = lax.axis_index("hx")
    half = value.shape[0] // 2
    slots = jnp.arange(nx)
    outs = []
    for way, part in ((1, value[:half]), (-1, value[half:])):
        pairs = [(src, (src + way) % nx) for src in range(nx)]
        got = [part]
        for step in range(nx - 1):
            got.append(lax.ppermute(got[-1], "hx", pairs))
        stacked = jnp.stack(got)
        outs.append(jnp.take(stacked, way * (x - slots) % nx, axis=0))
    return jnp.concatenate(outs, axis=1).reshape(nx * value.shape[0], value.shape[1])


def gather_z(value):
    nz = lax.axis_size("hz")
    copies = jnp.broadcast_to(value[None], (nz,) + value.shape)
    got = lax.all_to_all(copies, "hz", 0, 0, tiled=False)
    return got.reshape(nz * value.shape[0], value.shape[1])


def gather_over_head(value):
    return ring_gather_x(gather_z(value))


def normalize_rows(layer_sum, mlp_gain):
    mean_square = jnp.mean(layer_sum * layer_sum, axis=1, keepdims=True)
    return (layer_sum * lax.rsqrt(mean_square + epsilon) * mlp_gain).astype(jnp.bfloat16)


def shards(
    x_in,
    z_in,
    bc,
    dt_raw,
    dt_bias,
    decay_rate,
    d_skip,
    norm_gain,
    out_weight,
    resid,
    mlp_gain,
    gate_weight,
    up_weight,
    down_weight,
):
    out_full, down_full = (
        lax.all_gather(out_weight, SEQ, axis=1, tiled=True),
        lax.all_gather(down_weight, SEQ, axis=1, tiled=True),
    )
    head_count = dt_raw.shape[0]
    length = dt_raw.shape[1]
    head_width = x_in.shape[1] // head_count
    step_size = jax.nn.softplus(dt_raw + dt_bias[:, None])
    log_decay = -decay_rate[:, None] * step_size
    x_heads = x_in.reshape(length, head_count, head_width)
    local_out, local_state = block_scan(x_heads, bc[0], bc[1], step_size, log_decay, BLOCK)
    running = jnp.cumsum(log_decay, axis=1)
    group_decay = jnp.exp(running[:, -1])
    entering = entering_state(group_decay, local_state)
    carried = jnp.einsum(
        "tn,hpn->thp", bc[1].astype(jnp.float32), entering, precision=lax.Precision.HIGHEST
    )
    carried = carried * jnp.exp(running).T[:, :, None]
    ssd_out = local_out + carried + d_skip[None, :, None] * x_heads.astype(jnp.float32)
    gated_out = ssd_out.reshape(length, head_count * head_width) * jax.nn.silu(
        z_in.astype(jnp.float32)
    )
    row_squares = jnp.sum(gated_out * gated_out, axis=1)
    gated_scaled = (gated_out * norm_gain).astype(jnp.bfloat16)
    head_n = lax.axis_size("hx") * lax.axis_size("hz")
    chunks = 1
    rows_per = length // head_n // chunks
    width = out_full.shape[1]
    gated_parts = gated_scaled.reshape(head_n, chunks, rows_per, -1)
    square_parts = row_squares.reshape(head_n, chunks, rows_per)
    resid_parts = resid.reshape(chunks, rows_per, -1)

    def packed_rows(chunk):
        chunk_rows = gated_parts[:, chunk].reshape(head_n * rows_per, -1)
        chunk_squares = square_parts[:, chunk].reshape(head_n * rows_per)
        partial_value = jnp.dot(chunk_rows, out_full, preferred_element_type=jnp.float32)
        sq_hi = chunk_squares.astype(jnp.bfloat16)
        sq_lo = (chunk_squares - sq_hi.astype(jnp.float32)).astype(jnp.bfloat16)
        extra = (
            jnp.zeros((head_n * rows_per, 128), jnp.bfloat16)
            .at[:, 0]
            .set(sq_hi)
            .at[:, 1]
            .set(sq_lo)
        )
        return jnp.concatenate([partial_value.astype(jnp.bfloat16), extra], axis=1)

    def finish_rows(reduced, chunk):
        part_rows = reduced[:, :width]
        part_squares = reduced[:, width] + reduced[:, width + 1]
        layer_sum = (
            resid_parts[chunk].astype(jnp.float32)
            + part_rows * lax.rsqrt(part_squares / INNER + epsilon)[:, None]
        )
        return (layer_sum, normalize_rows(layer_sum, mlp_gain))

    def mlp_rows(rows_piece, down_full):
        gate_part = jnp.dot(rows_piece, gate_weight, preferred_element_type=jnp.float32)
        up_part = jnp.dot(rows_piece, up_weight, preferred_element_type=jnp.float32)
        hidden = (jax.nn.silu(gate_part) * up_part).astype(jnp.bfloat16)
        mlp_part = jnp.dot(hidden, down_full, preferred_element_type=jnp.float32)
        return sum_over_head(mlp_part.astype(jnp.bfloat16))

    packs = [packed_rows(chunk) for chunk in range(chunks)]
    normed_rows = []
    sums = []
    for chunk in range(chunks):
        pack = packs[chunk]
        if chunk > 0:
            pack, normed_rows[-1] = lax.optimization_barrier((pack, normed_rows[-1]))
        reduced = sum_over_head(pack)
        if chunk == 0:
            reduced, down_full = lax.optimization_barrier((reduced, down_full))
        layer_sum, normed = finish_rows(reduced, chunk)
        sums.append(layer_sum)
        normed_rows.append(normed)
    gathered = []
    for chunk in range(chunks):
        gathered.append(gather_over_head(normed_rows[chunk]))
        if chunk + 1 < chunks:
            gathered[-1], normed_rows[chunk + 1] = lax.optimization_barrier(
                (gathered[-1], normed_rows[chunk + 1])
            )
    outs = [sums[c] + mlp_rows(gathered[c], down_full) for c in range(chunks)]
    return jnp.concatenate(outs, axis=0).astype(jnp.bfloat16)


def solution(mesh):
    seq_n, head_n = mesh.devices.shape
    devices = mesh.devices.reshape(seq_n // 4, 2, 2, 4, head_n // 4)
    mesh = jax.sharding.Mesh(devices, ("sy", "sz", "sc", "hx", "hz"))
    head = ("hx", "hz")
    in_specs = (
        P(SEQ, head),
        P(SEQ, head),
        P(None, SEQ, None),
        P(head, SEQ),
        P(head),
        P(head),
        P(head),
        P(head),
        P(head, SEQ),
        P(SEQ + head, None),
        P(),
        P(None, head),
        P(None, head),
        P(head, SEQ),
    )
    out_specs = P(SEQ + head, None)
    return jax.shard_map(shards, mesh=mesh, in_specs=in_specs, out_specs=out_specs, check_vma=False)
```

profile of v0, /device:TPU:8, one launch (start us, length us, event | category | flops | bytes accessed | tf_op | source)
XLA Modules:
  0.0 354.5 jit_solution(17849686165738651231)
XLA Ops:
  6.5 0.7 all-gather.3.cloned.1.call-update
  8.0 0.8 broadcast_multiply_fusion
  10.3 1.1 fusion.73
  13.2 1.8 collective-permute-start.6
  15.0 1.1 reduce-window.26
  16.6 1.3 collective-permute-start
  17.9 0.9 fusion.53
  18.9 0.8 collective-permute-start.7
  20.0 1.2 fusion.5
  21.9 0.7 collective-permute-start.2
  22.6 0.7 collective-permute-start.8
  23.3 0.7 collective-permute-start.5
  23.9 0.7 collective-permute-start.4
  24.6 0.7 collective-permute-start.3
  25.4 0.7 collective-permute-start.11
  26.1 0.7 collective-permute-start.10
  26.8 0.7 collective-permute-start.9
  27.7 0.7 collective-permute-start.12
  28.8 0.7 compare_reduce_fusion.1
  29.5 0.7 compare_reduce_fusion
  30.3 1.8 convolution_bitcast_fusion.3
  32.0 0.8 collective-permute-start.13
  32.9 1.3 collective-permute-start.14
  34.2 0.7 fusion.4
  34.9 38.6 %collective-permute-done.14 = f32[8,64,128]{2,1,0:T(8,128)S(1)} collective-permute-done((f32[8,64,128]{2,1,0:T(8,128)S(1)}, f32[8,64,128]{2,1,0:T(8,128)S(1)}, u32[]{:S(2)}, u32[]{:S(2)}) %collective-permute-start.14) | collective-permute-done | bytes 262176 | tf_op jit(solution)/shard_map/ppermute | solution.py:58
  73.5 0.8 fusion.2
  74.7 0.7 copy-done.5
  76.0 1.4 fusion.40
  77.8 18.0 %all-gather.3.cloned.1.call-done = bf16[512,4096]{1,0:T(8,128)(2,1)} async-done(((bf16[512,256]{1,0:T(8,128)(2,1)}), bf16[512,4096]{1,0:T(8,128)(2,1)}) %all-gather.3.cloned.1.call-update) | async-done | bytes 4194320 | tf_op jit(solution)/shard_map/all_gather | solution.py:169
  95.8 4.6 %convolution_convert_fusion.1 = bf16[512,4096]{1,0:T(8,128)(2,1)S(1)} fusion(bf16[512,4096]{1,0:T(8,128)(2,1)} %all-gather.3.cloned.1.call-done, f32[512]{0:T(512)S(1)} %copy-done.16, f32[512,512]{1,0:T(8,128)S(1)} %copy.29, bf16[512,512]{1,0:T(8,128)(2,1)S(1)} %copy-done.5), kind=kOutput, calls=%fused_computation.3 | convolution fusion | flops 2151677952 | bytes 9963520 | tf_op jit(solution)/shard_map/dot_general | solution.py:203
  101.2 2.8 collective-permute-start.18
  104.3 11.6 %collective-permute-done.18 = bf16[4,16,4224]{2,1,0:T(8,128)(2,1)S(1)} collective-permute-done((bf16[4,16,4224]{2,1,0:T(8,128)(2,1)S(1)}, bf16[4,16,4224]{2,1,0:T(8,128)(2,1)S(1)}, u32[]{:S(2)}, u32[]{:S(2)}) %collective-permute-start.18) | collective-permute-done | bytes 540704 | tf_op jit(solution)/shard_map/ppermute | solution.py:105
  116.1 3.8 %collective-permute-start.19 = (bf16[4,16,4224]{2,1,0:T(8,128)(2,1)S(1)}, bf16[4,16,4224]{2,1,0:T(8,128)(2,1)S(1)}, u32[]{:S(2)}, u32[]{:S(2)}) collective-permute-start(bf16[4,16,4224]{2,1,0:T(8,128)(2,1)S(1)} %add_convert_fusion.2), channel_id=1, source_target_pairs={{0,12},{4,0},{8,4},{12,8},{1,13},{5,1},{9,5},{13,9},{2,14},{6,2},{... | collective-permute-start | bytes 1622024 | tf_op jit(solution)/shard_map/ppermute | solution.py:105
  120.1 10.8 %collective-permute-done.19 = bf16[4,16,4224]{2,1,0:T(8,128)(2,1)S(1)} collective-permute-done((bf16[4,16,4224]{2,1,0:T(8,128)(2,1)S(1)}, bf16[4,16,4224]{2,1,0:T(8,128)(2,1)S(1)}, u32[]{:S(2)}, u32[]{:S(2)}) %collective-permute-start.19) | collective-permute-done | bytes 540704 | tf_op jit(solution)/shard_map/ppermute | solution.py:105
  131.1 3.8 %collective-permute-start.20 = (bf16[4,16,4224]{2,1,0:T(8,128)(2,1)S(1)}, bf16[4,16,4224]{2,1,0:T(8,128)(2,1)S(1)}, u32[]{:S(2)}, u32[]{:S(2)}) collective-permute-start(bf16[4,16,4224]{2,1,0:T(8,128)(2,1)S(1)} %add_convert_fusion.1), channel_id=1, source_target_pairs={{0,12},{4,0},{8,4},{12,8},{1,13},{5,1},{9,5},{13,9},{2,14},{6,2},{... | collective-permute-start | bytes 1622024 | tf_op jit(solution)/shard_map/ppermute | solution.py:105
  135.2 10.0 %collective-permute-done.20 = bf16[4,16,4224]{2,1,0:T(8,128)(2,1)S(1)} collective-permute-done((bf16[4,16,4224]{2,1,0:T(8,128)(2,1)S(1)}, bf16[4,16,4224]{2,1,0:T(8,128)(2,1)S(1)}, u32[]{:S(2)}, u32[]{:S(2)}) %collective-permute-start.20) | collective-permute-done | bytes 540704 | tf_op jit(solution)/shard_map/ppermute | solution.py:105
  145.3 3.5 collective-permute-done.17
  149.1 34.4 %all_to_all.15 = bf16[4,32,4224]{2,1,0:T(8,128)(2,1)S(1)} all-to-all(bf16[4,32,4224]{2,1,0:T(8,128)(2,1)S(1)} %pad_maximum_fusion.4), channel_id=1, replica_groups=mesh['sy'=4,'sz'=2,'sc'=2,'hx'=4,'hz'=4] {'hz'}, dimensions={0} | all-to-all | bytes 2162688 | tf_op jit(solution)/shard_map/all_to_all | solution.py:116
  184.4 29.2 %all_to_all.16 = bf16[4,32,4096]{2,1,0:T(8,128)(2,1)S(1)} all-to-all(bf16[4,32,4096]{2,1,0:T(8,128)(2,1)S(1)} %broadcast_in_dim.42), channel_id=1, replica_groups=mesh['sy'=4,'sz'=2,'sc'=2,'hx'=4,'hz'=4] {'hz'}, dimensions={0} | all-to-all | bytes 2097152 | tf_op jit(solution)/shard_map/all_to_all | solution.py:139
  213.7 3.3 collective-permute-start.24
  217.0 10.5 %collective-permute-done.24 = bf16[64,4096]{1,0:T(8,128)(2,1)S(1)} collective-permute-done((bf16[64,4096]{1,0:T(8,128)(2,1)S(1)}, bf16[64,4096]{1,0:T(8,128)(2,1)S(1)}, u32[]{:S(2)}, u32[]{:S(2)}) %collective-permute-start.24) | collective-permute-done | bytes 524320 | tf_op jit(solution)/shard_map/ppermute | solution.py:130
  227.5 3.7 %collective-permute-start.25 = (bf16[64,4096]{1,0:T(8,128)(2,1)S(1)}, bf16[64,4096]{1,0:T(8,128)(2,1)S(1)}, u32[]{:S(2)}, u32[]{:S(2)}) collective-permute-start(bf16[64,4096]{1,0:T(8,128)(2,1)S(1)} %collective-permute-done.24), channel_id=1, source_target_pairs={{0,12},{4,0},{8,4},{12,8},{1,13},{5,1},{9,5},{13,9},{2,14},{6,2},{... | collective-permute-start | bytes 1572872 | tf_op jit(solution)/shard_map/ppermute | solution.py:130
  231.2 9.6 %collective-permute-done.25 = bf16[64,4096]{1,0:T(8,128)(2,1)S(1)} collective-permute-done((bf16[64,4096]{1,0:T(8,128)(2,1)S(1)}, bf16[64,4096]{1,0:T(8,128)(2,1)S(1)}, u32[]{:S(2)}, u32[]{:S(2)}) %collective-permute-start.25) | collective-permute-done | bytes 524320 | tf_op jit(solution)/shard_map/ppermute | solution.py:130
  240.8 3.7 %collective-permute-start.26 = (bf16[64,4096]{1,0:T(8,128)(2,1)S(1)}, bf16[64,4096]{1,0:T(8,128)(2,1)S(1)}, u32[]{:S(2)}, u32[]{:S(2)}) collective-permute-start(bf16[64,4096]{1,0:T(8,128)(2,1)S(1)} %collective-permute-done.25), channel_id=1, source_target_pairs={{0,12},{4,0},{8,4},{12,8},{1,13},{5,1},{9,5},{13,9},{2,14},{6,2},{... | collective-permute-start | bytes 1572872 | tf_op jit(solution)/shard_map/ppermute | solution.py:130
  244.9 8.4 %collective-permute-done.26 = bf16[64,4096]{1,0:T(8,128)(2,1)S(1)} collective-permute-done((bf16[64,4096]{1,0:T(8,128)(2,1)S(1)}, bf16[64,4096]{1,0:T(8,128)(2,1)S(1)}, u32[]{:S(2)}, u32[]{:S(2)}) %collective-permute-start.26) | collective-permute-done | bytes 524320 | tf_op jit(solution)/shard_map/ppermute | solution.py:130
  253.5 2.0 gather_fusion.1
  255.5 3.2 broadcast_select_fusion
  258.8 1.5 pad_maximum_fusion.2
  260.2 2.0 gather_fusion
  262.3 2.0 broadcast_select_fusion.1
  265.0 2.1 copy-done.1
  267.1 1.1 copy-done.15
  268.2 2.3 fusion.74
  270.5 11.2 %convolution_convert_fusion = bf16[512,4096]{1,0:T(8,128)(2,1)} fusion(bf16[512,4096]{1,0:T(8,128)(2,1)} %all-gather.5.cloned.1.call-done, bf16[512,4096]{1,0:T(8,128)(2,1)} %bitcast.126, bf16[4096,512]{1,0:T(8,128)(2,1)} %param.36, f32[512,512]{1,0:T(8,128)S(1)} %fusion.74), kind=kOutput, calls=%fused_computation.2 | convolution fusion | flops 4298637312 | bytes 17825792 | tf_op jit(solution)/shard_map/dot_general | solution.py:228
  281.7 2.7 fusion.71
  284.5 3.8 %collective-permute-start.30 = (bf16[4,16,4096]{2,1,0:T(8,128)(2,1)S(1)}, bf16[4,16,4096]{2,1,0:T(8,128)(2,1)S(1)}, u32[]{:S(2)}, u32[]{:S(2)}) collective-permute-start(bf16[4,16,4096]{2,1,0:T(8,128)(2,1)S(1)} %select_bitcast_fusion.2), channel_id=1, source_target_pairs={{0,12},{4,0},{8,4},{12,8},{1,13},{5,1},{9,5},{13,9},{2,14},{6,2},{... | collective-permute-start | bytes 1572872 | tf_op jit(solution)/shard_map/ppermute | solution.py:105
  288.5 8.0 %collective-permute-done.30 = bf16[4,16,4096]{2,1,0:T(8,128)(2,1)S(1)} collective-permute-done((bf16[4,16,4096]{2,1,0:T(8,128)(2,1)S(1)}, bf16[4,16,4096]{2,1,0:T(8,128)(2,1)S(1)}, u32[]{:S(2)}, u32[]{:S(2)}) %collective-permute-start.30) | collective-permute-done | bytes 524320 | tf_op jit(solution)/shard_map/ppermute | solution.py:105
  296.6 3.8 %collective-permute-start.31 = (bf16[4,16,4096]{2,1,0:T(8,128)(2,1)S(1)}, bf16[4,16,4096]{2,1,0:T(8,128)(2,1)S(1)}, u32[]{:S(2)}, u32[]{:S(2)}) collective-permute-start(bf16[4,16,4096]{2,1,0:T(8,128)(2,1)S(1)} %add_convert_fusion.8), channel_id=1, source_target_pairs={{0,12},{4,0},{8,4},{12,8},{1,13},{5,1},{9,5},{13,9},{2,14},{6,2},{... | collective-permute-start | bytes 1572872 | tf_op jit(solution)/shard_map/ppermute | solution.py:105
  300.6 7.9 %collective-permute-done.31 = bf16[4,16,4096]{2,1,0:T(8,128)(2,1)S(1)} collective-permute-done((bf16[4,16,4096]{2,1,0:T(8,128)(2,1)S(1)}, bf16[4,16,4096]{2,1,0:T(8,128)(2,1)S(1)}, u32[]{:S(2)}, u32[]{:S(2)}) %collective-permute-start.31) | collective-permute-done | bytes 524320 | tf_op jit(solution)/shard_map/ppermute | solution.py:105
  308.7 3.8 %collective-permute-start.32 = (bf16[4,16,4096]{2,1,0:T(8,128)(2,1)S(1)}, bf16[4,16,4096]{2,1,0:T(8,128)(2,1)S(1)}, u32[]{:S(2)}, u32[]{:S(2)}) collective-permute-start(bf16[4,16,4096]{2,1,0:T(8,128)(2,1)S(1)} %add_convert_fusion.7), channel_id=1, source_target_pairs={{0,12},{4,0},{8,4},{12,8},{1,13},{5,1},{9,5},{13,9},{2,14},{6,2},{... | collective-permute-start | bytes 1572872 | tf_op jit(solution)/shard_map/ppermute | solution.py:105
  312.7 6.4 %collective-permute-done.32 = bf16[4,16,4096]{2,1,0:T(8,128)(2,1)S(1)} collective-permute-done((bf16[4,16,4096]{2,1,0:T(8,128)(2,1)S(1)}, bf16[4,16,4096]{2,1,0:T(8,128)(2,1)S(1)}, u32[]{:S(2)}, u32[]{:S(2)}) %collective-permute-start.32) | collective-permute-done | bytes 524320 | tf_op jit(solution)/shard_map/ppermute | solution.py:105
  319.3 3.8 %collective-permute-done.29 = bf16[4,16,4096]{2,1,0:T(8,128)(2,1)S(1)} collective-permute-done((bf16[4,16,4096]{2,1,0:T(8,128)(2,1)S(1)}, bf16[4,16,4096]{2,1,0:T(8,128)(2,1)S(1)}, u32[]{:S(2)}, u32[]{:S(2)}) %collective-permute-start.29) | collective-permute-done | bytes 524320 | tf_op jit(solution)/shard_map/ppermute | solution.py:105
  323.4 23.3 %all_to_all.17 = bf16[4,32,4096]{2,1,0:T(8,128)(2,1)S(1)} all-to-all(bf16[4,32,4096]{2,1,0:T(8,128)(2,1)S(1)} %pad_maximum_fusion.5), channel_id=1, replica_groups=mesh['sy'=4,'sz'=2,'sc'=2,'hx'=4,'hz'=4] {'hz'}, dimensions={0} | all-to-all | bytes 2097152 | tf_op jit(solution)/shard_map/all_to_all | solution.py:116
  346.8 0.8 add_convert_fusion.12
  (141 shorter events, 13.5 us)
Async XLA Ops:
  6.5 5.6 %copy-start.4 = (bf16[2,512,128]{2,1,0:T(8,128)(2,1)S(1)}, bf16[2,512,128]{2,1,0:T(8,128)(2,1)}, u32[]{:S(2)}) copy-start(bf16[2,512,128]{2,1,0:T(8,128)(2,1)} %param.26) | copy-start | bytes 786436
  6.5 89.2 %all-gather.3.cloned.1.call-start = ((), (), s32[]{:S(2)}) async-start(), calls=%async_computation.3 | async-start | bytes 4456448 | tf_op jit(solution)/shard_map/all_gather | solution.py:169
  7.3 176.4 %all-gather.5.cloned.1.call-start = ((), (), s32[]{:S(2)}) async-start(), calls=%async_computation.4 | async-start | bytes 4456448 | tf_op jit(solution)/shard_map/all_gather | solution.py:170
  11.7 1.0 copy-start.9
  13.2 5.6 %collective-permute-start.6 = (f32[8,64,128]{2,1,0:T(8,128)S(1)}, f32[8,64,128]{2,1,0:T(8,128)S(1)}, u32[]{:S(2)}, u32[]{:S(2)}) collective-permute-start(f32[8,64,128]{2,1,0:T(8,128)S(1)} %fusion.6), channel_id=1, source_target_pairs={{0,16},{32,48},{1,17},{33,49},{2,18},{34,50},{3,19},{35,51},{4,20}... | collective-permute-start | bytes 786440 | tf_op jit(solution)/shard_map/ppermute | solution.py:58
  16.6 4.6 %collective-permute-start = (f32[8]{0:T(128)S(1)}, f32[8]{0:T(128)S(1)}, u32[]{:S(2)}, u32[]{:S(2)}) collective-permute-start(f32[8]{0:T(128)S(1)} %fusion.61), channel_id=1, source_target_pairs={{0,16},{32,48},{1,17},{33,49},{2,18},{34,50},{3,19},{35,51},{4,20}... | collective-permute-start | bytes 104 | tf_op jit(solution)/shard_map/ppermute | solution.py:58
  18.8 9.7 %copy-start.3 = (bf16[512,512]{1,0:T(8,128)(2,1)S(1)}, bf16[512,512]{1,0:T(8,128)(2,1)}, u32[]{:S(2)}) copy-start(bf16[512,512]{1,0:T(8,128)(2,1)} %param.24) | copy-start | bytes 1572868
  18.9 3.6 %collective-permute-start.7 = (f32[8,64,128]{2,1,0:T(8,128)S(1)}, f32[8,64,128]{2,1,0:T(8,128)S(1)}, u32[]{:S(2)}, u32[]{:S(2)}) collective-permute-start(f32[8,64,128]{2,1,0:T(8,128)S(1)} %multiply_add_fusion.2), channel_id=1, source_target_pairs={{16,32},{17,33},{18,34},{19,35},{20,36},{21,37},{22,38},{23,39},{2... | collective-permute-start | bytes 786440 | tf_op jit(solution)/shard_map/ppermute | solution.py:58
  21.2 0.7 collective-permute-start.1
  21.9 1.4 collective-permute-start.2
  22.5 6.0 %copy-start.10 = (f32[8,64,128]{2,1,0:T(8,128)}, f32[8,64,128]{2,1,0:T(8,128)S(1)}, u32[]{:S(2)}) copy-start(f32[8,64,128]{2,1,0:T(8,128)S(1)} %collective-permute-done.7) | copy-start | bytes 786436
  22.6 2.7 collective-permute-start.8
  23.3 2.0 collective-permute-start.5
  23.9 3.5 collective-permute-start.4
  24.6 2.9 collective-permute-start.3
  25.4 2.1 collective-permute-start.11
  26.1 1.4 collective-permute-start.10
  26.8 0.8 collective-permute-start.9
  27.7 5.2 %collective-permute-start.12 = (f32[8,64,128]{2,1,0:T(8,128)S(1)}, f32[8,64,128]{2,1,0:T(8,128)S(1)}, u32[]{:S(2)}, u32[]{:S(2)}) collective-permute-start(f32[8,64,128]{2,1,0:T(8,128)S(1)} %select_add_fusion), channel_id=1, source_target_pairs={{48,16},{49,17},{50,18},{51,19},{52,20},{53,21},{54,22},{55,23},{5... | collective-permute-start | bytes 786440 | tf_op jit(solution)/shard_map/ppermute | solution.py:58
  28.8 5.4 %copy-start.6 = (f32[256,8,64]{0,2,1:T(8,128)S(1)}, f32[256,8,64]{0,2,1:T(8,128)}, u32[]{:S(2)}) copy-start(f32[256,8,64]{0,2,1:T(8,128)} %fusion.5) | copy-start | bytes 1572868
  32.0 41.5 %copy-start.11 = (f32[8,64,128]{2,1,0:T(8,128)S(1)}, f32[8,64,128]{2,1,0:T(8,128)}, u32[]{:S(2)}) copy-start(f32[8,64,128]{2,1,0:T(8,128)} %copy-done.10) | copy-start | bytes 786436
  32.0 41.5 %copy-start.14 = (f32[8]{0:T(128)S(1)}, f32[8]{0:T(128)}, u32[]{:S(2)}) copy-start(f32[8]{0:T(128)} %param.30) | copy-start | bytes 100
  32.0 2.9 collective-permute-start.13
  32.9 40.7 %copy-start.12 = (f32[8,64,128]{2,1,0:T(8,128)}, f32[8,64,128]{2,1,0:T(8,128)S(1)}, u32[]{:S(2)}) copy-start(f32[8,64,128]{2,1,0:T(8,128)S(1)} %collective-permute-done.12) | copy-start | bytes 786436
  32.9 40.7 %collective-permute-start.14 = (f32[8,64,128]{2,1,0:T(8,128)S(1)}, f32[8,64,128]{2,1,0:T(8,128)S(1)}, u32[]{:S(2)}, u32[]{:S(2)}) collective-permute-start(f32[8,64,128]{2,1,0:T(8,128)S(1)} %collective-permute-done.12), channel_id=1, source_target_pairs={{16,0},{17,1},{18,2},{19,3},{20,4},{21,5},{22,6},{23,7},{24,8},{25... | collective-permute-start | bytes 786440 | tf_op jit(solution)/shard_map/ppermute | solution.py:58
  74.3 1.0 copy-start.5
  74.3 21.4 %copy-start.16 = (f32[512]{0:T(512)S(1)}, f32[512]{0:T(512)}, u32[]{:S(2)}) copy-start(f32[512]{0:T(512)} %param.31) | copy-start | bytes 6148
  101.2 14.7 %collective-permute-start.18 = (bf16[4,16,4224]{2,1,0:T(8,128)(2,1)S(1)}, bf16[4,16,4224]{2,1,0:T(8,128)(2,1)S(1)}, u32[]{:S(2)}, u32[]{:S(2)}) collective-permute-start(bf16[4,16,4224]{2,1,0:T(8,128)(2,1)S(1)} %select_bitcast_fusion), channel_id=1, source_target_pairs={{0,12},{4,0},{8,4},{12,8},{1,13},{5,1},{9,5},{13,9},{2,14},{6,2},{... | collective-permute-start | bytes 1622024 | tf_op jit(solution)/shard_map/ppermute | solution.py:105
  104.0 15.8 %collective-permute-start.15 = (bf16[4,16,4224]{2,1,0:T(8,128)(2,1)S(1)}, bf16[4,16,4224]{2,1,0:T(8,128)(2,1)S(1)}, u32[]{:S(2)}, u32[]{:S(2)}) collective-permute-start(bf16[4,16,4224]{2,1,0:T(8,128)(2,1)S(1)} %select_bitcast_fusion.1), channel_id=1, source_target_pairs={{0,4},{4,8},{8,12},{12,0},{1,5},{5,9},{9,13},{13,1},{2,6},{6,10},{... | collective-permute-start | bytes 1622024 | tf_op jit(solution)/shard_map/ppermute | solution.py:105
  116.1 14.9 %collective-permute-start.19 = (bf16[4,16,4224]{2,1,0:T(8,128)(2,1)S(1)}, bf16[4,16,4224]{2,1,0:T(8,128)(2,1)S(1)}, u32[]{:S(2)}, u32[]{:S(2)}) collective-permute-start(bf16[4,16,4224]{2,1,0:T(8,128)(2,1)S(1)} %add_convert_fusion.2), channel_id=1, source_target_pairs={{0,12},{4,0},{8,4},{12,8},{1,13},{5,1},{9,5},{13,9},{2,14},{6,2},{... | collective-permute-start | bytes 1622024 | tf_op jit(solution)/shard_map/ppermute | solution.py:105
  120.0 14.9 %collective-permute-start.16 = (bf16[4,16,4224]{2,1,0:T(8,128)(2,1)S(1)}, bf16[4,16,4224]{2,1,0:T(8,128)(2,1)S(1)}, u32[]{:S(2)}, u32[]{:S(2)}) collective-permute-start(bf16[4,16,4224]{2,1,0:T(8,128)(2,1)S(1)} %add_convert_fusion.5), channel_id=1, source_target_pairs={{0,4},{4,8},{8,12},{12,0},{1,5},{5,9},{9,13},{13,1},{2,6},{6,10},{... | collective-permute-start | bytes 1622024 | tf_op jit(solution)/shard_map/ppermute | solution.py:105
  131.1 14.0 %collective-permute-start.20 = (bf16[4,16,4224]{2,1,0:T(8,128)(2,1)S(1)}, bf16[4,16,4224]{2,1,0:T(8,128)(2,1)S(1)}, u32[]{:S(2)}, u32[]{:S(2)}) collective-permute-start(bf16[4,16,4224]{2,1,0:T(8,128)(2,1)S(1)} %add_convert_fusion.1), channel_id=1, source_target_pairs={{0,12},{4,0},{8,4},{12,8},{1,13},{5,1},{9,5},{13,9},{2,14},{6,2},{... | collective-permute-start | bytes 1622024 | tf_op jit(solution)/shard_map/ppermute | solution.py:105
  135.1 13.7 %collective-permute-start.17 = (bf16[4,16,4224]{2,1,0:T(8,128)(2,1)S(1)}, bf16[4,16,4224]{2,1,0:T(8,128)(2,1)S(1)}, u32[]{:S(2)}, u32[]{:S(2)}) collective-permute-start(bf16[4,16,4224]{2,1,0:T(8,128)(2,1)S(1)} %add_convert_fusion.4), channel_id=1, source_target_pairs={{0,4},{4,8},{8,12},{12,0},{1,5},{5,9},{9,13},{13,1},{2,6},{6,10},{... | collective-permute-start | bytes 1622024 | tf_op jit(solution)/shard_map/ppermute | solution.py:105
  149.1 34.8 %copy-start.2 = (bf16[32,4096]{1,0:T(8,128)(2,1)S(1)}, bf16[32,4096]{1,0:T(8,128)(2,1)}, u32[]{:S(2)}) copy-start(bf16[32,4096]{1,0:T(8,128)(2,1)} %param.33) | copy-start | bytes 786436
  149.1 35.0 %copy-start.13 = (f32[4096]{0:T(1024)S(1)}, f32[4096]{0:T(1024)}, u32[]{:S(2)}) copy-start(f32[4096]{0:T(1024)} %param.34) | copy-start | bytes 49156
  213.7 13.8 %collective-permute-start.24 = (bf16[64,4096]{1,0:T(8,128)(2,1)S(1)}, bf16[64,4096]{1,0:T(8,128)(2,1)S(1)}, u32[]{:S(2)}, u32[]{:S(2)}) collective-permute-start(bf16[64,4096]{1,0:T(8,128)(2,1)S(1)} %bitcast.131), channel_id=1, source_target_pairs={{0,12},{4,0},{8,4},{12,8},{1,13},{5,1},{9,5},{13,9},{2,14},{6,2},{... | collective-permute-start | bytes 1572872 | tf_op jit(solution)/shard_map/ppermute | solution.py:130
  217.0 14.2 %collective-permute-start.21 = (bf16[64,4096]{1,0:T(8,128)(2,1)S(1)}, bf16[64,4096]{1,0:T(8,128)(2,1)S(1)}, u32[]{:S(2)}, u32[]{:S(2)}) collective-permute-start(bf16[64,4096]{1,0:T(8,128)(2,1)S(1)} %bitcast.129), channel_id=1, source_target_pairs={{0,4},{4,8},{8,12},{12,0},{1,5},{5,9},{9,13},{13,1},{2,6},{6,10},{... | collective-permute-start | bytes 1572872 | tf_op jit(solution)/shard_map/ppermute | solution.py:130
  227.5 13.3 %collective-permute-start.25 = (bf16[64,4096]{1,0:T(8,128)(2,1)S(1)}, bf16[64,4096]{1,0:T(8,128)(2,1)S(1)}, u32[]{:S(2)}, u32[]{:S(2)}) collective-permute-start(bf16[64,4096]{1,0:T(8,128)(2,1)S(1)} %collective-permute-done.24), channel_id=1, source_target_pairs={{0,12},{4,0},{8,4},{12,8},{1,13},{5,1},{9,5},{13,9},{2,14},{6,2},{... | collective-permute-start | bytes 1572872 | tf_op jit(solution)/shard_map/ppermute | solution.py:130
  231.2 22.1 %copy-start.7 = (bf16[64,4096]{1,0:T(8,128)(2,1)}, bf16[64,4096]{1,0:T(8,128)(2,1)S(1)}, u32[]{:S(2)}) copy-start(bf16[64,4096]{1,0:T(8,128)(2,1)S(1)} %collective-permute-done.21) | copy-start | bytes 1572868
  231.2 13.4 %collective-permute-start.22 = (bf16[64,4096]{1,0:T(8,128)(2,1)S(1)}, bf16[64,4096]{1,0:T(8,128)(2,1)}, u32[]{:S(2)}, u32[]{:S(2)}) collective-permute-start(bf16[64,4096]{1,0:T(8,128)(2,1)S(1)} %collective-permute-done.21), channel_id=1, source_target_pairs={{0,4},{4,8},{8,12},{12,0},{1,5},{5,9},{9,13},{13,1},{2,6},{6,10},{... | collective-permute-start | bytes 1572872 | tf_op jit(solution)/shard_map/ppermute | solution.py:130
  240.8 12.5 %collective-permute-start.26 = (bf16[64,4096]{1,0:T(8,128)(2,1)S(1)}, bf16[64,4096]{1,0:T(8,128)(2,1)S(1)}, u32[]{:S(2)}, u32[]{:S(2)}) collective-permute-start(bf16[64,4096]{1,0:T(8,128)(2,1)S(1)} %collective-permute-done.25), channel_id=1, source_target_pairs={{0,12},{4,0},{8,4},{12,8},{1,13},{5,1},{9,5},{13,9},{2,14},{6,2},{... | collective-permute-start | bytes 1572872 | tf_op jit(solution)/shard_map/ppermute | solution.py:130
  244.6 14.2 %collective-permute-start.23 = (bf16[64,4096]{1,0:T(8,128)(2,1)}, bf16[64,4096]{1,0:T(8,128)(2,1)}, u32[]{:S(2)}, u32[]{:S(2)}) collective-permute-start(bf16[64,4096]{1,0:T(8,128)(2,1)} %collective-permute-done.22), channel_id=1, source_target_pairs={{0,4},{4,8},{8,12},{12,0},{1,5},{5,9},{9,13},{13,1},{2,6},{6,10},{... | collective-permute-start | bytes 1572872 | tf_op jit(solution)/shard_map/ppermute | solution.py:130
  255.5 3.2 copy-start.8
  262.3 2.2 copy-start
  264.5 3.7 %copy-start.15 = (bf16[4096,512]{1,0:T(8,128)(2,1)S(1)}, bf16[4096,512]{1,0:T(8,128)(2,1)}, u32[]{:S(2)}) copy-start(bf16[4096,512]{1,0:T(8,128)(2,1)} %param.35) | copy-start | bytes 12582916
  265.0 2.1 copy-start.1
  284.5 11.9 %collective-permute-start.30 = (bf16[4,16,4096]{2,1,0:T(8,128)(2,1)S(1)}, bf16[4,16,4096]{2,1,0:T(8,128)(2,1)S(1)}, u32[]{:S(2)}, u32[]{:S(2)}) collective-permute-start(bf16[4,16,4096]{2,1,0:T(8,128)(2,1)S(1)} %select_bitcast_fusion.2), channel_id=1, source_target_pairs={{0,12},{4,0},{8,4},{12,8},{1,13},{5,1},{9,5},{13,9},{2,14},{6,2},{... | collective-permute-start | bytes 1572872 | tf_op jit(solution)/shard_map/ppermute | solution.py:105
  288.4 12.0 %collective-permute-start.27 = (bf16[4,16,4096]{2,1,0:T(8,128)(2,1)S(1)}, bf16[4,16,4096]{2,1,0:T(8,128)(2,1)S(1)}, u32[]{:S(2)}, u32[]{:S(2)}) collective-permute-start(bf16[4,16,4096]{2,1,0:T(8,128)(2,1)S(1)} %select_bitcast_fusion.3), channel_id=1, source_target_pairs={{0,4},{4,8},{8,12},{12,0},{1,5},{5,9},{9,13},{13,1},{2,6},{6,10},{... | collective-permute-start | bytes 1572872 | tf_op jit(solution)/shard_map/ppermute | solution.py:105
  296.6 11.9 %collective-permute-start.31 = (bf16[4,16,4096]{2,1,0:T(8,128)(2,1)S(1)}, bf16[4,16,4096]{2,1,0:T(8,128)(2,1)S(1)}, u32[]{:S(2)}, u32[]{:S(2)}) collective-permute-start(bf16[4,16,4096]{2,1,0:T(8,128)(2,1)S(1)} %add_convert_fusion.8), channel_id=1, source_target_pairs={{0,12},{4,0},{8,4},{12,8},{1,13},{5,1},{9,5},{13,9},{2,14},{6,2},{... | collective-permute-start | bytes 1572872 | tf_op jit(solution)/shard_map/ppermute | solution.py:105
  300.6 11.9 %collective-permute-start.28 = (bf16[4,16,4096]{2,1,0:T(8,128)(2,1)S(1)}, bf16[4,16,4096]{2,1,0:T(8,128)(2,1)S(1)}, u32[]{:S(2)}, u32[]{:S(2)}) collective-permute-start(bf16[4,16,4096]{2,1,0:T(8,128)(2,1)S(1)} %add_convert_fusion.11), channel_id=1, source_target_pairs={{0,4},{4,8},{8,12},{12,0},{1,5},{5,9},{9,13},{13,1},{2,6},{6,10},{... | collective-permute-start | bytes 1572872 | tf_op jit(solution)/shard_map/ppermute | solution.py:105
  308.7 10.5 %collective-permute-start.32 = (bf16[4,16,4096]{2,1,0:T(8,128)(2,1)S(1)}, bf16[4,16,4096]{2,1,0:T(8,128)(2,1)S(1)}, u32[]{:S(2)}, u32[]{:S(2)}) collective-permute-start(bf16[4,16,4096]{2,1,0:T(8,128)(2,1)S(1)} %add_convert_fusion.7), channel_id=1, source_target_pairs={{0,12},{4,0},{8,4},{12,8},{1,13},{5,1},{9,5},{13,9},{2,14},{6,2},{... | collective-permute-start | bytes 1572872 | tf_op jit(solution)/shard_map/ppermute | solution.py:105
  312.6 10.5 %collective-permute-start.29 = (bf16[4,16,4096]{2,1,0:T(8,128)(2,1)S(1)}, bf16[4,16,4096]{2,1,0:T(8,128)(2,1)S(1)}, u32[]{:S(2)}, u32[]{:S(2)}) collective-permute-start(bf16[4,16,4096]{2,1,0:T(8,128)(2,1)S(1)} %add_convert_fusion.10), channel_id=1, source_target_pairs={{0,4},{4,8},{8,12},{12,0},{1,5},{5,9},{9,13},{13,1},{2,6},{6,10},{... | collective-permute-start | bytes 1572872 | tf_op jit(solution)/shard_map/ppermute | solution.py:105
Sparse Core Ops, SparseCore 0:
  9.9 85.8 all-gather.2
  98.3 78.7 all-gather.4
where the time goes:
time: 355 us; the launch traced here: 354 us
  waiting for transfers between devices  148 us (42%)
  blocking collectives  86.8 us (24%)
  starting transfers between devices  46 us (13%)
  matrix products  24.8 us (7%)
  other arithmetic  20 us (6%)
  local copies, waits for them, and re-layouts  14.6 us (4%)
  between operations  14.5 us (4%)
    ppermute x12, waiting for transfers between devices, ring_sum_x(): got = lax.ppermute(acc.astype(jnp.bfloat16), 'hx', pairs)  62.1 us
    all_to_all x2, blocking collectives, sum_over_head(): pieces = lax.all_to_all(pieces, 'hz', 0, 0, tiled=False)  57.6 us
    ppermute x15, waiting for transfers between devices, send(): return tuple((lax.ppermute(v, axes, pairs) for v in pair))  38.6 us
    all_to_all x1, blocking collectives, gather_z(): got = lax.all_to_all(copies, 'hz', 0, 0, tiled=False)  29.2 us
    ppermute x6, waiting for transfers between devices, ring_gather_x(): got.append(lax.ppermute(got[-1], 'hx', pairs))  28.5 us
    ppermute x12, starting transfers between devices, ring_sum_x(): got = lax.ppermute(acc.astype(jnp.bfloat16), 'hx', pairs)  22.3 us
    all_gather x1, waiting for transfers between devices, shards(): lax.all_gather(out_weight, SEQ, axis=1, tiled=True)  18 us
    ppermute x15, starting transfers between devices, send(): return tuple((lax.ppermute(v, axes, pairs) for v in pair))  12.6 us
  transfers between devices with their start and end apart: 35, of which 13 were waited for; matrix products, arithmetic and copies ran while one was open for 9% of the time, Pallas kernels for 0%

commit v1 on v0

--- a/solution.py
+++ b/solution.py
@@ -166,7 +166,9 @@
     down_weight,
 ):
     out_full, down_full = (
-        lax.all_gather(out_weight, SEQ, axis=1, tiled=True),
+        jnp.concatenate(
+            lax.all_to_all(jnp.stack([out_weight] * lax.axis_size(SEQ)), SEQ, 0, 0), axis=1
+        ),
         lax.all_gather(down_weight, SEQ, axis=1, tiled=True),
     )
     head_count = dt_raw.shape[0]

time: 355 us -> 434 us (1.22)
  waiting for transfers between devices: 148 us -> 197 us
  blocking collectives: 86.8 us -> 104 us
  starting transfers between devices: 46 us -> 53.7 us
    ppermute x15, waiting for transfers between devices: 38.6 us -> 103 us  [send(): return tuple((lax.ppermute(v, axes, pairs) for v in pair))]
    all_to_all x2, blocking collectives: 57.6 us -> 76.7 us  [sum_over_head(): pieces = lax.all_to_all(pieces, 'hz', 0, 0, tiled=False)]
    all_gather x1 -> x0, waiting for transfers between devices: 18 us -> none  [shards(): lax.all_gather(out_weight, SEQ, axis=1, tiled=True)]
    all_to_all x0 -> x1, starting transfers between devices: none -> 11.7 us  [shards(): lax.all_to_all(jnp.stack([out_weight] * lax.axis_size(SEQ)), SEQ, 0, 0)]
  transfers between devices with their start and end apart: 35 -> 35, of which waited for: 13 -> 13; matrix products, arithmetic and copies ran while one was open for 9% -> 7% of each run, Pallas kernels for 0% -> 0%
where the time goes in v1:
time: 434 us; the launch traced here: 429 us
  waiting for transfers between devices  197 us (45%)
  blocking collectives  104 us (24%)
  starting transfers between devices  53.7 us (12%)
  matrix products  24.8 us (6%)
  other arithmetic  18.5 us (4%)
  local copies, waits for them, and re-layouts  17 us (4%)
  between operations  14.5 us (3%)
    ppermute x15, waiting for transfers between devices, send(): return tuple((lax.ppermute(v, axes, pairs) for v in pair))  103 us
    all_to_all x2, blocking collectives, sum_over_head(): pieces = lax.all_to_all(pieces, 'hz', 0, 0, tiled=False)  76.7 us
    ppermute x12, waiting for transfers between devices, ring_sum_x(): got = lax.ppermute(acc.astype(jnp.bfloat16), 'hx', pairs)  65 us
    ppermute x6, waiting for transfers between devices, ring_gather_x(): got.append(lax.ppermute(got[-1], 'hx', pairs))  28.2 us
    all_to_all x1, blocking collectives, gather_z(): got = lax.all_to_all(copies, 'hz', 0, 0, tiled=False)  27.5 us
    ppermute x12, starting transfers between devices, ring_sum_x(): got = lax.ppermute(acc.astype(jnp.bfloat16), 'hx', pairs)  22.2 us
    ppermute x15, starting transfers between devices, send(): return tuple((lax.ppermute(v, axes, pairs) for v in pair))  12.8 us
    all_to_all x1, starting transfers between devices, shards(): lax.all_to_all(jnp.stack([out_weight] * lax.axis_size(SEQ)), SEQ, 0, 0)  11.7 us
  transfers between devices with their start and end apart: 35, of which 13 were waited for; matrix products, arithmetic and copies ran while one was open for 7% of the time, Pallas kernels for 0%

profile of v1, /device:TPU:8, one launch (start us, length us, event | category | flops | bytes accessed | tf_op | source)
XLA Modules:
  0.0 429.4 jit_solution(1620267550536280314)
XLA Ops:
  6.5 1.1 copy.31
  7.6 2.4 stack.22
  10.0 11.7 %all-to-all-start = ((bf16[16,512,256]{1,2,0:T(8,128)(2,1)}), bf16[16,512,256]{1,2,0:T(8,128)(2,1)}, u32[]{:S(2)}, u32[]{:S(2)}) async-start(bf16[16,512,256]{1,2,0:T(8,128)(2,1)} %stack.22), calls=%async_computation | async-start | bytes 8388608 | tf_op jit(solution)/shard_map/all_to_all | solution.py:170
  21.8 0.7 all-gather.2.cloned.1.call-update
  26.0 2.0 collective-permute-start.6
  28.1 1.1 reduce-window.26
  29.7 1.3 collective-permute-start
  31.0 0.9 fusion.53
  32.0 0.7 collective-permute-start.7
  32.9 1.2 fusion.5
  34.8 0.7 collective-permute-start.2
  35.5 0.7 collective-permute-start.8
  36.2 0.7 collective-permute-start.5
  36.8 0.7 collective-permute-start.4
  37.5 0.7 collective-permute-start.3
  38.3 0.7 collective-permute-start.11
  39.0 0.7 collective-permute-start.10
  39.7 0.7 collective-permute-start.9
  40.6 0.7 collective-permute-start.12
  41.7 0.7 compare_reduce_fusion.1
  42.4 0.7 compare_reduce_fusion
  43.1 1.7 convolution_bitcast_fusion.3
  44.9 0.8 collective-permute-start.13
  45.7 1.3 collective-permute-start.14
  47.1 0.7 fusion.4
  47.8 102.8 %collective-permute-done.14 = f32[8,64,128]{2,1,0:T(8,128)S(1)} collective-permute-done((f32[8,64,128]{2,1,0:T(8,128)S(1)}, f32[8,64,128]{2,1,0:T(8,128)S(1)}, u32[]{:S(2)}, u32[]{:S(2)}) %collective-permute-start.14) | collective-permute-done | bytes 262176 | tf_op jit(solution)/shard_map/ppermute | solution.py:58
  150.6 0.8 fusion.2
  151.8 0.7 copy-done.5
  153.0 1.3 fusion.40
  154.8 4.7 %convolution_convert_fusion.1 = bf16[512,4096]{1,0:T(8,128)(2,1)S(1)} fusion(bf16[512,4096]{0,1:T(8,128)(2,1)} %bitcast.26, f32[512]{0:T(512)S(1)} %copy-done.18, f32[512,512]{1,0:T(8,128)S(1)} %copy.30, bf16[512,512]{1,0:T(8,128)(2,1)S(1)} %copy-done.5), kind=kOutput, calls=%fused_computation.3 | convolution fusion | flops 2151677952 | bytes 9963520 | tf_op jit(solution)/shard_map/dot_general | solution.py:205
  160.3 2.8 collective-permute-start.18
  163.5 12.3 %collective-permute-done.18 = bf16[4,16,4224]{2,1,0:T(8,128)(2,1)S(1)} collective-permute-done((bf16[4,16,4224]{2,1,0:T(8,128)(2,1)S(1)}, bf16[4,16,4224]{2,1,0:T(8,128)(2,1)S(1)}, u32[]{:S(2)}, u32[]{:S(2)}) %collective-permute-start.18) | collective-permute-done | bytes 540704 | tf_op jit(solution)/shard_map/ppermute | solution.py:105
  175.9 3.8 collective-permute-start.19
  179.9 11.6 %collective-permute-done.19 = bf16[4,16,4224]{2,1,0:T(8,128)(2,1)S(1)} collective-permute-done((bf16[4,16,4224]{2,1,0:T(8,128)(2,1)S(1)}, bf16[4,16,4224]{2,1,0:T(8,128)(2,1)S(1)}, u32[]{:S(2)}, u32[]{:S(2)}) %collective-permute-start.19) | collective-permute-done | bytes 540704 | tf_op jit(solution)/shard_map/ppermute | solution.py:105
  191.7 3.8 collective-permute-start.20
  195.7 10.7 %collective-permute-done.20 = bf16[4,16,4224]{2,1,0:T(8,128)(2,1)S(1)} collective-permute-done((bf16[4,16,4224]{2,1,0:T(8,128)(2,1)S(1)}, bf16[4,16,4224]{2,1,0:T(8,128)(2,1)S(1)}, u32[]{:S(2)}, u32[]{:S(2)}) %collective-permute-start.20) | collective-permute-done | bytes 540704 | tf_op jit(solution)/shard_map/ppermute | solution.py:105
  206.6 3.5 collective-permute-done.17
  210.3 53.2 %all_to_all.20 = bf16[4,32,4224]{2,1,0:T(8,128)(2,1)S(1)} all-to-all(bf16[4,32,4224]{2,1,0:T(8,128)(2,1)S(1)} %pad_maximum_fusion.4), channel_id=1, replica_groups=mesh['sy'=4,'sz'=2,'sc'=2,'hx'=4,'hz'=4] {'hz'}, dimensions={0} | all-to-all | bytes 2162688 | tf_op jit(solution)/shard_map/all_to_all | solution.py:116
  264.5 27.5 %all_to_all.21 = bf16[4,32,4096]{2,1,0:T(8,128)(2,1)S(1)} all-to-all(bf16[4,32,4096]{2,1,0:T(8,128)(2,1)S(1)} %broadcast_in_dim.42), channel_id=1, replica_groups=mesh['sy'=4,'sz'=2,'sc'=2,'hx'=4,'hz'=4] {'hz'}, dimensions={0} | all-to-all | bytes 2097152 | tf_op jit(solution)/shard_map/all_to_all | solution.py:139
  292.6 1.5 collective-permute-start.21
  294.1 10.4 %collective-permute-done.24 = bf16[64,4096]{1,0:T(8,128)(2,1)S(1)} collective-permute-done((bf16[64,4096]{1,0:T(8,128)(2,1)S(1)}, bf16[64,4096]{1,0:T(8,128)(2,1)S(1)}, u32[]{:S(2)}, u32[]{:S(2)}) %collective-permute-start.24) | collective-permute-done | bytes 524320 | tf_op jit(solution)/shard_map/ppermute | solution.py:130
  304.5 1.7 collective-permute-start.25
  306.5 9.9 %collective-permute-done.25 = bf16[64,4096]{1,0:T(8,128)(2,1)S(1)} collective-permute-done((bf16[64,4096]{1,0:T(8,128)(2,1)S(1)}, bf16[64,4096]{1,0:T(8,128)(2,1)S(1)}, u32[]{:S(2)}, u32[]{:S(2)}) %collective-permute-start.25) | collective-permute-done | bytes 524320 | tf_op jit(solution)/shard_map/ppermute | solution.py:130
  316.5 2.5 collective-permute-start.26
  319.4 7.9 %collective-permute-done.26 = bf16[64,4096]{1,0:T(8,128)(2,1)S(1)} collective-permute-done((bf16[64,4096]{1,0:T(8,128)(2,1)S(1)}, bf16[64,4096]{1,0:T(8,128)(2,1)S(1)}, u32[]{:S(2)}, u32[]{:S(2)}) %collective-permute-start.26) | collective-permute-done | bytes 524320 | tf_op jit(solution)/shard_map/ppermute | solution.py:130
  327.5 2.0 gather_fusion.1
  329.5 3.2 broadcast_select_fusion
  332.8 1.5 pad_maximum_fusion.2
  334.2 2.0 gather_fusion
  336.3 2.0 broadcast_select_fusion.1
  339.0 2.1 copy-done.1
  341.1 1.1 copy-done.17
  342.2 2.3 fusion.74
  344.5 11.2 %convolution_convert_fusion = bf16[512,4096]{1,0:T(8,128)(2,1)} fusion(bf16[512,4096]{1,0:T(8,128)(2,1)} %all-gather.2.cloned.1.call-done, bf16[512,4096]{1,0:T(8,128)(2,1)} %bitcast.129, bf16[4096,512]{1,0:T(8,128)(2,1)} %param.36, f32[512,512]{1,0:T(8,128)S(1)} %fusion.74), kind=kOutput, calls=%fused_computation.2 | convolution fusion | flops 4298637312 | bytes 17825792 | tf_op jit(solution)/shard_map/dot_general | solution.py:230
  355.8 2.7 fusion.71
  358.5 3.7 collective-permute-start.30
  362.4 8.0 %collective-permute-done.30 = bf16[4,16,4096]{2,1,0:T(8,128)(2,1)S(1)} collective-permute-done((bf16[4,16,4096]{2,1,0:T(8,128)(2,1)S(1)}, bf16[4,16,4096]{2,1,0:T(8,128)(2,1)S(1)}, u32[]{:S(2)}, u32[]{:S(2)}) %collective-permute-start.30) | collective-permute-done | bytes 524320 | tf_op jit(solution)/shard_map/ppermute | solution.py:105
  370.5 3.8 collective-permute-start.31
  374.6 8.4 %collective-permute-done.31 = bf16[4,16,4096]{2,1,0:T(8,128)(2,1)S(1)} collective-permute-done((bf16[4,16,4096]{2,1,0:T(8,128)(2,1)S(1)}, bf16[4,16,4096]{2,1,0:T(8,128)(2,1)S(1)}, u32[]{:S(2)}, u32[]{:S(2)}) %collective-permute-start.31) | collective-permute-done | bytes 524320 | tf_op jit(solution)/shard_map/ppermute | solution.py:105
  383.1 3.8 collective-permute-start.32
  387.4 6.2 %collective-permute-done.32 = bf16[4,16,4096]{2,1,0:T(8,128)(2,1)S(1)} collective-permute-done((bf16[4,16,4096]{2,1,0:T(8,128)(2,1)S(1)}, bf16[4,16,4096]{2,1,0:T(8,128)(2,1)S(1)}, u32[]{:S(2)}, u32[]{:S(2)}) %collective-permute-start.32) | collective-permute-done | bytes 524320 | tf_op jit(solution)/shard_map/ppermute | solution.py:105
  393.8 4.1 collective-permute-done.29
  398.1 23.5 %all_to_all.22 = bf16[4,32,4096]{2,1,0:T(8,128)(2,1)S(1)} all-to-all(bf16[4,32,4096]{2,1,0:T(8,128)(2,1)S(1)} %pad_maximum_fusion.5), channel_id=1, replica_groups=mesh['sy'=4,'sz'=2,'sc'=2,'hx'=4,'hz'=4] {'hz'}, dimensions={0} | all-to-all | bytes 2097152 | tf_op jit(solution)/shard_map/all_to_all | solution.py:116
  421.7 0.8 add_convert_fusion.12
  (148 shorter events, 14.2 us)
Async XLA Ops:
  10.0 12.5 %copy-start.19 = (f32[8]{0:T(128)S(1)}, f32[8]{0:T(128)}, u32[]{:S(2)}) copy-start(f32[8]{0:T(128)} %param.29) | copy-start | bytes 100
  10.0 12.5 %copy-start.14 = (f32[8,512]{1,0:T(8,128)S(1)}, f32[8,512]{1,0:T(8,128)}, u32[]{:S(2)}) copy-start(f32[8,512]{1,0:T(8,128)} %param.27) | copy-start | bytes 49156
  10.0 12.5 %copy-start.15 = (f32[8]{0:T(128)S(1)}, f32[8]{0:T(128)}, u32[]{:S(2)}) copy-start(f32[8]{0:T(128)} %param.28) | copy-start | bytes 100
  10.0 14.2 %copy-start.3 = (bf16[512,512]{1,0:T(8,128)(2,1)S(1)}, bf16[512,512]{1,0:T(8,128)(2,1)}, u32[]{:S(2)}) copy-start(bf16[512,512]{1,0:T(8,128)(2,1)} %param.24) | copy-start | bytes 1572868
  10.0 144.8 %all-to-all-start = ((bf16[16,512,256]{1,2,0:T(8,128)(2,1)}), bf16[16,512,256]{1,2,0:T(8,128)(2,1)}, u32[]{:S(2)}, u32[]{:S(2)}) async-start(bf16[16,512,256]{1,2,0:T(8,128)(2,1)} %stack.22), calls=%async_computation | async-start | bytes 8388608 | tf_op jit(solution)/shard_map/all_to_all | solution.py:170
  21.7 3.3 copy-start.4
  21.7 242.0 %all-gather.2.cloned.1.call-start = ((), (), s32[]{:S(2)}) async-start(), calls=%async_computation.4 | async-start | bytes 4456448 | tf_op jit(solution)/shard_map/all_gather | solution.py:172
  24.5 1.0 copy-start.9
  26.0 5.9 %collective-permute-start.6 = (f32[8,64,128]{2,1,0:T(8,128)S(1)}, f32[8,64,128]{2,1,0:T(8,128)S(1)}, u32[]{:S(2)}, u32[]{:S(2)}) collective-permute-start(f32[8,64,128]{2,1,0:T(8,128)S(1)} %fusion.6), channel_id=1, source_target_pairs={{0,16},{32,48},{1,17},{33,49},{2,18},{34,50},{3,19},{35,51},{4,20}... | collective-permute-start | bytes 786440 | tf_op jit(solution)/shard_map/ppermute | solution.py:58
  29.7 4.4 %collective-permute-start = (f32[8]{0:T(128)S(1)}, f32[8]{0:T(128)S(1)}, u32[]{:S(2)}, u32[]{:S(2)}) collective-permute-start(f32[8]{0:T(128)S(1)} %fusion.61), channel_id=1, source_target_pairs={{0,16},{32,48},{1,17},{33,49},{2,18},{34,50},{3,19},{35,51},{4,20}... | collective-permute-start | bytes 104 | tf_op jit(solution)/shard_map/ppermute | solution.py:58
  32.0 3.4 collective-permute-start.7
  34.1 0.7 collective-permute-start.1
  34.8 1.4 collective-permute-start.2
  35.5 6.0 %copy-start.10 = (f32[8,64,128]{2,1,0:T(8,128)}, f32[8,64,128]{2,1,0:T(8,128)S(1)}, u32[]{:S(2)}) copy-start(f32[8,64,128]{2,1,0:T(8,128)S(1)} %collective-permute-done.7) | copy-start | bytes 786436
  35.5 2.7 collective-permute-start.8
  36.2 2.0 collective-permute-start.5
  36.8 3.5 collective-permute-start.4
  37.5 2.9 collective-permute-start.3
  38.3 2.1 collective-permute-start.11
  39.0 1.4 collective-permute-start.10
  39.7 0.8 collective-permute-start.9
  40.6 5.1 %collective-permute-start.12 = (f32[8,64,128]{2,1,0:T(8,128)S(1)}, f32[8,64,128]{2,1,0:T(8,128)S(1)}, u32[]{:S(2)}, u32[]{:S(2)}) collective-permute-start(f32[8,64,128]{2,1,0:T(8,128)S(1)} %select_add_fusion), channel_id=1, source_target_pairs={{48,16},{49,17},{50,18},{51,19},{52,20},{53,21},{54,22},{55,23},{5... | collective-permute-start | bytes 786440 | tf_op jit(solution)/shard_map/ppermute | solution.py:58
  41.7 5.3 %copy-start.6 = (f32[256,8,64]{0,2,1:T(8,128)S(1)}, f32[256,8,64]{0,2,1:T(8,128)}, u32[]{:S(2)}) copy-start(f32[256,8,64]{0,2,1:T(8,128)} %fusion.5) | copy-start | bytes 1572868
  44.9 105.7 %copy-start.11 = (f32[8,64,128]{2,1,0:T(8,128)S(1)}, f32[8,64,128]{2,1,0:T(8,128)}, u32[]{:S(2)}) copy-start(f32[8,64,128]{2,1,0:T(8,128)} %copy-done.10) | copy-start | bytes 786436
  44.9 105.7 %copy-start.16 = (f32[8]{0:T(128)S(1)}, f32[8]{0:T(128)}, u32[]{:S(2)}) copy-start(f32[8]{0:T(128)} %param.30) | copy-start | bytes 100
  44.9 2.9 collective-permute-start.13
  45.7 104.9 %copy-start.12 = (f32[8,64,128]{2,1,0:T(8,128)}, f32[8,64,128]{2,1,0:T(8,128)S(1)}, u32[]{:S(2)}) copy-start(f32[8,64,128]{2,1,0:T(8,128)S(1)} %collective-permute-done.12) | copy-start | bytes 786436
  45.7 104.8 %collective-permute-start.14 = (f32[8,64,128]{2,1,0:T(8,128)S(1)}, f32[8,64,128]{2,1,0:T(8,128)S(1)}, u32[]{:S(2)}, u32[]{:S(2)}) collective-permute-start(f32[8,64,128]{2,1,0:T(8,128)S(1)} %collective-permute-done.12), channel_id=1, source_target_pairs={{16,0},{17,1},{18,2},{19,3},{20,4},{21,5},{22,6},{23,7},{24,8},{25... | collective-permute-start | bytes 786440 | tf_op jit(solution)/shard_map/ppermute | solution.py:58
  151.4 1.0 copy-start.5
  151.4 3.4 copy-start.18
  160.3 15.4 %collective-permute-start.18 = (bf16[4,16,4224]{2,1,0:T(8,128)(2,1)S(1)}, bf16[4,16,4224]{2,1,0:T(8,128)(2,1)S(1)}, u32[]{:S(2)}, u32[]{:S(2)}) collective-permute-start(bf16[4,16,4224]{2,1,0:T(8,128)(2,1)S(1)} %select_bitcast_fusion), channel_id=1, source_target_pairs={{0,12},{4,0},{8,4},{12,8},{1,13},{5,1},{9,5},{13,9},{2,14},{6,2},{... | collective-permute-start | bytes 1622024 | tf_op jit(solution)/shard_map/ppermute | solution.py:105
  163.2 16.5 %collective-permute-start.15 = (bf16[4,16,4224]{2,1,0:T(8,128)(2,1)S(1)}, bf16[4,16,4224]{2,1,0:T(8,128)(2,1)S(1)}, u32[]{:S(2)}, u32[]{:S(2)}) collective-permute-start(bf16[4,16,4224]{2,1,0:T(8,128)(2,1)S(1)} %select_bitcast_fusion.1), channel_id=1, source_target_pairs={{0,4},{4,8},{8,12},{12,0},{1,5},{5,9},{9,13},{13,1},{2,6},{6,10},{... | collective-permute-start | bytes 1622024 | tf_op jit(solution)/shard_map/ppermute | solution.py:105
  175.9 15.6 %collective-permute-start.19 = (bf16[4,16,4224]{2,1,0:T(8,128)(2,1)S(1)}, bf16[4,16,4224]{2,1,0:T(8,128)(2,1)S(1)}, u32[]{:S(2)}, u32[]{:S(2)}) collective-permute-start(bf16[4,16,4224]{2,1,0:T(8,128)(2,1)S(1)} %add_convert_fusion.2), channel_id=1, source_target_pairs={{0,12},{4,0},{8,4},{12,8},{1,13},{5,1},{9,5},{13,9},{2,14},{6,2},{... | collective-permute-start | bytes 1622024 | tf_op jit(solution)/shard_map/ppermute | solution.py:105
  179.9 15.6 %collective-permute-start.16 = (bf16[4,16,4224]{2,1,0:T(8,128)(2,1)S(1)}, bf16[4,16,4224]{2,1,0:T(8,128)(2,1)S(1)}, u32[]{:S(2)}, u32[]{:S(2)}) collective-permute-start(bf16[4,16,4224]{2,1,0:T(8,128)(2,1)S(1)} %add_convert_fusion.5), channel_id=1, source_target_pairs={{0,4},{4,8},{8,12},{12,0},{1,5},{5,9},{9,13},{13,1},{2,6},{6,10},{... | collective-permute-start | bytes 1622024 | tf_op jit(solution)/shard_map/ppermute | solution.py:105
  191.7 14.7 %collective-permute-start.20 = (bf16[4,16,4224]{2,1,0:T(8,128)(2,1)S(1)}, bf16[4,16,4224]{2,1,0:T(8,128)(2,1)S(1)}, u32[]{:S(2)}, u32[]{:S(2)}) collective-permute-start(bf16[4,16,4224]{2,1,0:T(8,128)(2,1)S(1)} %add_convert_fusion.1), channel_id=1, source_target_pairs={{0,12},{4,0},{8,4},{12,8},{1,13},{5,1},{9,5},{13,9},{2,14},{6,2},{... | collective-permute-start | bytes 1622024 | tf_op jit(solution)/shard_map/ppermute | solution.py:105
  195.6 14.4 %collective-permute-start.17 = (bf16[4,16,4224]{2,1,0:T(8,128)(2,1)S(1)}, bf16[4,16,4224]{2,1,0:T(8,128)(2,1)S(1)}, u32[]{:S(2)}, u32[]{:S(2)}) collective-permute-start(bf16[4,16,4224]{2,1,0:T(8,128)(2,1)S(1)} %add_convert_fusion.4), channel_id=1, source_target_pairs={{0,4},{4,8},{8,12},{12,0},{1,5},{5,9},{9,13},{13,1},{2,6},{6,10},{... | collective-permute-start | bytes 1622024 | tf_op jit(solution)/shard_map/ppermute | solution.py:105
  210.3 53.6 %copy-start.2 = (bf16[32,4096]{1,0:T(8,128)(2,1)S(1)}, bf16[32,4096]{1,0:T(8,128)(2,1)}, u32[]{:S(2)}) copy-start(bf16[32,4096]{1,0:T(8,128)(2,1)} %param.33) | copy-start | bytes 786436
  210.3 53.9 %copy-start.13 = (f32[4096]{0:T(1024)S(1)}, f32[4096]{0:T(1024)}, u32[]{:S(2)}) copy-start(f32[4096]{0:T(1024)} %param.34) | copy-start | bytes 49156
  292.0 12.5 %collective-permute-start.24 = (bf16[64,4096]{1,0:T(8,128)(2,1)S(1)}, bf16[64,4096]{1,0:T(8,128)(2,1)S(1)}, u32[]{:S(2)}, u32[]{:S(2)}) collective-permute-start(bf16[64,4096]{1,0:T(8,128)(2,1)S(1)} %bitcast.134), channel_id=1, source_target_pairs={{0,12},{4,0},{8,4},{12,8},{1,13},{5,1},{9,5},{13,9},{2,14},{6,2},{... | collective-permute-start | bytes 1572872 | tf_op jit(solution)/shard_map/ppermute | solution.py:130
  292.6 13.6 %collective-permute-start.21 = (bf16[64,4096]{1,0:T(8,128)(2,1)S(1)}, bf16[64,4096]{1,0:T(8,128)(2,1)S(1)}, u32[]{:S(2)}, u32[]{:S(2)}) collective-permute-start(bf16[64,4096]{1,0:T(8,128)(2,1)S(1)} %bitcast.132), channel_id=1, source_target_pairs={{0,4},{4,8},{8,12},{12,0},{1,5},{5,9},{9,13},{13,1},{2,6},{6,10},{... | collective-permute-start | bytes 1572872 | tf_op jit(solution)/shard_map/ppermute | solution.py:130
  304.5 12.0 %collective-permute-start.25 = (bf16[64,4096]{1,0:T(8,128)(2,1)S(1)}, bf16[64,4096]{1,0:T(8,128)(2,1)S(1)}, u32[]{:S(2)}, u32[]{:S(2)}) collective-permute-start(bf16[64,4096]{1,0:T(8,128)(2,1)S(1)} %collective-permute-done.24), channel_id=1, source_target_pairs={{0,12},{4,0},{8,4},{12,8},{1,13},{5,1},{9,5},{13,9},{2,14},{6,2},{... | collective-permute-start | bytes 1572872 | tf_op jit(solution)/shard_map/ppermute | solution.py:130
  306.2 21.1 %copy-start.7 = (bf16[64,4096]{1,0:T(8,128)(2,1)}, bf16[64,4096]{1,0:T(8,128)(2,1)S(1)}, u32[]{:S(2)}) copy-start(bf16[64,4096]{1,0:T(8,128)(2,1)S(1)} %collective-permute-done.21) | copy-start | bytes 1572868
  306.2 12.8 %collective-permute-start.22 = (bf16[64,4096]{1,0:T(8,128)(2,1)S(1)}, bf16[64,4096]{1,0:T(8,128)(2,1)}, u32[]{:S(2)}, u32[]{:S(2)}) collective-permute-start(bf16[64,4096]{1,0:T(8,128)(2,1)S(1)} %collective-permute-done.21), channel_id=1, source_target_pairs={{0,4},{4,8},{8,12},{12,0},{1,5},{5,9},{9,13},{13,1},{2,6},{6,10},{... | collective-permute-start | bytes 1572872 | tf_op jit(solution)/shard_map/ppermute | solution.py:130
  316.5 10.8 %collective-permute-start.26 = (bf16[64,4096]{1,0:T(8,128)(2,1)S(1)}, bf16[64,4096]{1,0:T(8,128)(2,1)S(1)}, u32[]{:S(2)}, u32[]{:S(2)}) collective-permute-start(bf16[64,4096]{1,0:T(8,128)(2,1)S(1)} %collective-permute-done.25), channel_id=1, source_target_pairs={{0,12},{4,0},{8,4},{12,8},{1,13},{5,1},{9,5},{13,9},{2,14},{6,2},{... | collective-permute-start | bytes 1572872 | tf_op jit(solution)/shard_map/ppermute | solution.py:130
  319.0 13.7 %collective-permute-start.23 = (bf16[64,4096]{1,0:T(8,128)(2,1)}, bf16[64,4096]{1,0:T(8,128)(2,1)}, u32[]{:S(2)}, u32[]{:S(2)}) collective-permute-start(bf16[64,4096]{1,0:T(8,128)(2,1)} %collective-permute-done.22), channel_id=1, source_target_pairs={{0,4},{4,8},{8,12},{12,0},{1,5},{5,9},{9,13},{13,1},{2,6},{6,10},{... | collective-permute-start | bytes 1572872 | tf_op jit(solution)/shard_map/ppermute | solution.py:130
  329.5 3.2 copy-start.8
  336.3 2.2 copy-start
  338.5 3.7 copy-start.17
  339.0 2.1 copy-start.1
  358.5 11.8 %collective-permute-start.30 = (bf16[4,16,4096]{2,1,0:T(8,128)(2,1)S(1)}, bf16[4,16,4096]{2,1,0:T(8,128)(2,1)S(1)}, u32[]{:S(2)}, u32[]{:S(2)}) collective-permute-start(bf16[4,16,4096]{2,1,0:T(8,128)(2,1)S(1)} %select_bitcast_fusion.2), channel_id=1, source_target_pairs={{0,12},{4,0},{8,4},{12,8},{1,13},{5,1},{9,5},{13,9},{2,14},{6,2},{... | collective-permute-start | bytes 1572872 | tf_op jit(solution)/shard_map/ppermute | solution.py:105
  362.3 12.0 %collective-permute-start.27 = (bf16[4,16,4096]{2,1,0:T(8,128)(2,1)S(1)}, bf16[4,16,4096]{2,1,0:T(8,128)(2,1)S(1)}, u32[]{:S(2)}, u32[]{:S(2)}) collective-permute-start(bf16[4,16,4096]{2,1,0:T(8,128)(2,1)S(1)} %select_bitcast_fusion.3), channel_id=1, source_target_pairs={{0,4},{4,8},{8,12},{12,0},{1,5},{5,9},{9,13},{13,1},{2,6},{6,10},{... | collective-permute-start | bytes 1572872 | tf_op jit(solution)/shard_map/ppermute | solution.py:105
  370.5 12.4 %collective-permute-start.31 = (bf16[4,16,4096]{2,1,0:T(8,128)(2,1)S(1)}, bf16[4,16,4096]{2,1,0:T(8,128)(2,1)S(1)}, u32[]{:S(2)}, u32[]{:S(2)}) collective-permute-start(bf16[4,16,4096]{2,1,0:T(8,128)(2,1)S(1)} %add_convert_fusion.8), channel_id=1, source_target_pairs={{0,12},{4,0},{8,4},{12,8},{1,13},{5,1},{9,5},{13,9},{2,14},{6,2},{... | collective-permute-start | bytes 1572872 | tf_op jit(solution)/shard_map/ppermute | solution.py:105
  374.5 12.7 %collective-permute-start.28 = (bf16[4,16,4096]{2,1,0:T(8,128)(2,1)S(1)}, bf16[4,16,4096]{2,1,0:T(8,128)(2,1)S(1)}, u32[]{:S(2)}, u32[]{:S(2)}) collective-permute-start(bf16[4,16,4096]{2,1,0:T(8,128)(2,1)S(1)} %add_convert_fusion.11), channel_id=1, source_target_pairs={{0,4},{4,8},{8,12},{12,0},{1,5},{5,9},{9,13},{13,1},{2,6},{6,10},{... | collective-permute-start | bytes 1572872 | tf_op jit(solution)/shard_map/ppermute | solution.py:105
  383.1 10.5 %collective-permute-start.32 = (bf16[4,16,4096]{2,1,0:T(8,128)(2,1)S(1)}, bf16[4,16,4096]{2,1,0:T(8,128)(2,1)S(1)}, u32[]{:S(2)}, u32[]{:S(2)}) collective-permute-start(bf16[4,16,4096]{2,1,0:T(8,128)(2,1)S(1)} %add_convert_fusion.7), channel_id=1, source_target_pairs={{0,12},{4,0},{8,4},{12,8},{1,13},{5,1},{9,5},{13,9},{2,14},{6,2},{... | collective-permute-start | bytes 1572872 | tf_op jit(solution)/shard_map/ppermute | solution.py:105
  387.3 10.5 %collective-permute-start.29 = (bf16[4,16,4096]{2,1,0:T(8,128)(2,1)S(1)}, bf16[4,16,4096]{2,1,0:T(8,128)(2,1)S(1)}, u32[]{:S(2)}, u32[]{:S(2)}) collective-permute-start(bf16[4,16,4096]{2,1,0:T(8,128)(2,1)S(1)} %add_convert_fusion.10), channel_id=1, source_target_pairs={{0,4},{4,8},{8,12},{12,0},{1,5},{5,9},{9,13},{13,1},{2,6},{6,10},{... | collective-permute-start | bytes 1572872 | tf_op jit(solution)/shard_map/ppermute | solution.py:105
Sparse Core Ops, SparseCore 0:
  25.1 141.3 all-gather.1
